TPU v7x, 32 devices: a whole 2x2x4 slice. The times are simulated.
32 devices in a mesh: expert: 8 (over z, x), tensor: 4 (over y, core).
Axes of the slice: x: 2, y: 2, z: 4, core: 2. Of those that a mesh axis runs over, the one named last changes fastest.
Arguments:
- context: bfloat16 [2048, 2048], P('expert', 'tensor'), may hold values from -0.25976562 to 0.25976562
- out_proj: bfloat16 [2048, 2048], P('tensor'), may hold values from -0.125 to 0.125
- residual: bfloat16 [2048, 2048], P(('expert', 'tensor')), may hold values from -0.25976562 to 0.25976562
- norm_gain: float32 [2048], replicated, may hold values from 0.1 to 1.9
- router_weight: float32 [2048, 64], replicated, may hold values from -5.524272 to 5.524272
- expert_ids: int32 [2048, 8], P('expert'), may hold values from 0 to 63, all different within a row; in each aligned block of 64 rows (0 to 63, 64 to 127, ...) at most 10 rows name the same one
- placement: int32 [128], replicated, may hold values from 0 to 63, as said below
- expert_weights: bfloat16 [128, 3, 2048, 1024], P('expert', None, None, 'tensor'), as said below
- post_gain: float32 [2048], replicated, may hold values from 0.5 to 1.5
Outputs:
- hidden_out: float32 [2048, 2048], P(('expert', 'tensor'))
- normed_out: float32 [2048, 2048], P(('expert', 'tensor'))
Inputs may be any that keep to these rules, and one draw needn't show every extreme that they name: `expert_ids`: each row names 8 different experts. In each aligned block of 64 rows (the rows of one device) no expert is named by more than 10 rows, a bound that some block reaches; every expert is named somewhere. `placement`: every expert is held by one, three or five slots. `expert_weights`: slots that hold the same expert carry equal weights.
All inputs are finite; a program needn't handle non-finite values.
Results may differ from a plain program's by a relative error of at most 0.018.
Values may be sent and summed in bfloat16 or wider, within the bound.
No kernel may reach another device: no remote copies, remote signals or barrier semaphores. Data moves between devices by JAX's collectives and lax.ppermute only.
A program may use at most 256 MiB of HBM per device.

v0:
```python
import jax
import jax.numpy as jnp
from jax import lax
from jax.sharding import PartitionSpec as P

EPS = 1e-06


def rms_scale(values, gain_row):
    mean_square = jnp.mean(values * values, axis=-1, keepdims=True)
    return values * lax.rsqrt(mean_square + EPS) * gain_row


def expert_inner(block_rows, weights):
    both_pre = jnp.einsum(
        "nqsmd,scdf->nqsmcf", block_rows, weights[:, :2], preferred_element_type=jnp.float32
    )
    return jax.nn.silu(both_pre[..., 0, :]) * both_pre[..., 1, :]


def expert_down(inner_act, weights):
    return jnp.einsum(
        "nqsmf,sdf->nqsmd", inner_act, weights[:, 2], preferred_element_type=jnp.float32
    )


def on_device(
    context,
    out_proj,
    residual,
    norm_gain,
    router_weight,
    expert_ids,
    placement,
    expert_weights,
    post_gain,
):
    groups = lax.axis_size("tensor")
    holders = lax.axis_size("expert")
    my_group = lax.axis_index("tensor")
    my_holder = lax.axis_index("expert")
    row_count = residual.shape[0]
    model_width = residual.shape[1]
    top_count = expert_ids.shape[1]
    expert_count = router_weight.shape[1]
    slot_dev = expert_weights.shape[0]
    slot_total = placement.shape[0]
    blocks = holders * groups
    capacity = max(2, row_count * top_count * 5 // (expert_count * 4))
    expert_range = jnp.arange(expert_count, dtype=jnp.int32)
    slot_range = jnp.arange(slot_total, dtype=jnp.int32)
    attention_parts = lax.all_to_all(
        jnp.dot(context, out_proj, preferred_element_type=jnp.float32)
        .astype(jnp.bfloat16)
        .reshape(groups, row_count, -1),
        "tensor",
        split_axis=0,
        concat_axis=0,
        tiled=True,
    )
    attention = jnp.sum(attention_parts.astype(jnp.float32), axis=0)
    hidden_mid = residual.astype(jnp.float32) + attention
    normed_full = rms_scale(hidden_mid, norm_gain)
    normed = normed_full.astype(jnp.bfloat16)
    logits = jnp.dot(normed_full, router_weight, precision=lax.Precision.HIGHEST)
    own_ids = lax.dynamic_slice_in_dim(expert_ids, my_group * row_count, row_count, 0)
    own_onehot = own_ids[:, :, None] == expert_range[None, None, :]
    chosen = jnp.sum(jnp.where(own_onehot, logits[:, None, :], 0.0), axis=-1)
    gate_weights = jax.nn.softmax(chosen, axis=-1)
    gate_hi = gate_weights.astype(jnp.bfloat16)
    gate_lo = (gate_weights - gate_hi.astype(jnp.float32)).astype(jnp.bfloat16)
    side = jnp.concatenate([own_ids.astype(jnp.bfloat16), gate_hi, gate_lo], axis=1)
    side = jnp.pad(side, ((0, 0), (0, 128 - 3 * top_count)))
    packed = lax.all_gather(
        jnp.concatenate([normed, side], axis=1), ("expert", "tensor"), axis=0, tiled=True
    ).reshape(blocks, row_count, model_width + 128)
    all_rows = packed[:, :, :model_width]
    all_ids = packed[:, :, model_width : model_width + top_count].astype(jnp.int32)
    all_hi = packed[:, :, model_width + top_count : model_width + 2 * top_count]
    all_lo = packed[:, :, model_width + 2 * top_count : model_width + 3 * top_count]
    holds = (placement[None, :] == expert_range[:, None]).astype(jnp.int32)
    copies = jnp.sum(holds, axis=1)
    copy_rank = jnp.cumsum(holds, axis=1) - 1
    holder_range = jnp.arange(holders, dtype=jnp.int32)
    copy_pick = holder_range[:, None] % copies[None, :]
    picked = (holds[None] > 0) & (copy_rank[None] == copy_pick[:, :, None])
    slot_pick = jnp.sum(jnp.where(picked, slot_range[None, None, :], 0), axis=2)
    local_range = jnp.arange(slot_dev, dtype=jnp.int32)
    mine_map = (slot_pick[:, :, None] == my_holder * slot_dev + local_range).astype(jnp.bfloat16)
    block_holder = jnp.arange(blocks, dtype=jnp.int32) // groups
    block_map = mine_map[block_holder]
    names = all_ids[:, :, :, None] == expert_range
    name_hot = jnp.any(names, axis=2).astype(jnp.bfloat16)
    gate_e_hi = jnp.sum(jnp.where(names, all_hi[:, :, :, None], 0), axis=2).astype(jnp.bfloat16)
    gate_e_lo = jnp.sum(jnp.where(names, all_lo[:, :, :, None], 0), axis=2).astype(jnp.bfloat16)
    stack = jnp.concatenate([name_hot, gate_e_hi, gate_e_lo], axis=1)
    per_slot = jnp.einsum("bue,bes->bus", stack, block_map, preferred_element_type=jnp.float32)
    token_hit = per_slot[:, :row_count]
    gate_sel_hi = per_slot[:, row_count : 2 * row_count]
    gate_sel_lo = per_slot[:, 2 * row_count :]
    token_range = jnp.arange(row_count, dtype=jnp.int32)
    earlier = (token_range[None, :] < token_range[:, None]).astype(jnp.bfloat16)
    count_before = jnp.einsum(
        "uv,bvs->bus", earlier, token_hit.astype(jnp.bfloat16), preferred_element_type=jnp.float32
    )
    rank_range = jnp.arange(capacity, dtype=jnp.float32)
    pick = token_hit[..., None] * (count_before[..., None] == rank_range)
    pick_hot = pick.astype(jnp.bfloat16)
    received = (
        jnp.einsum("busr,bud->bsrd", pick_hot, all_rows, preferred_element_type=jnp.float32)
        .astype(jnp.bfloat16)
        .reshape(holders, groups, slot_dev, capacity, model_width)
    )
    inner_f32 = expert_inner(received, expert_weights)
    if blocks * row_count * model_width * 4 <= 32 << 20:
        gate_sel = gate_sel_hi + gate_sel_lo
        pair_gate = jnp.sum(pick * gate_sel[..., None], axis=1)
        pair_gate = pair_gate.reshape(holders, groups, slot_dev, capacity, 1)
        inner_act = (inner_f32 * pair_gate).astype(jnp.bfloat16)
        partial_value = expert_down(inner_act, expert_weights).astype(jnp.bfloat16)
        partial_value = partial_value.reshape(blocks, slot_dev, capacity, model_width)
        combined = jnp.einsum(
            "hqusr,hqsrd->qhud",
            pick_hot.reshape(holders, groups, row_count, slot_dev, capacity),
            partial_value.reshape(holders, groups, slot_dev, capacity, model_width),
            preferred_element_type=jnp.float32,
        )
        moe_sum = lax.psum_scatter(
            combined.astype(jnp.bfloat16).reshape(-1, model_width),
            "tensor",
            scatter_dimension=0,
            tiled=True,
        ).reshape(holders, row_count, model_width)
        moe_sum = lax.all_to_all(moe_sum, "expert", split_axis=0, concat_axis=0, tiled=True)
        moe_sum = jnp.sum(moe_sum.astype(jnp.float32), axis=0)
    else:
        partial_value = expert_down(inner_f32.astype(jnp.bfloat16), expert_weights).astype(
            jnp.bfloat16
        )
        expert_sum = lax.psum_scatter(partial_value, "tensor", scatter_dimension=1, tiled=True)
        returned = lax.all_to_all(expert_sum, "expert", split_axis=0, concat_axis=0, tiled=True)
        own_flat = own_ids.reshape(-1)
        own_onehot_flat = own_flat[:, None] == expert_range
        slot_of = jnp.sum(jnp.where(own_onehot_flat, slot_pick[my_holder][None, :], 0), axis=-1)
        slot_hot = (slot_of[:, None] == slot_range).astype(jnp.int32)
        rank_in = jnp.sum(jnp.cumsum(slot_hot, axis=0) * slot_hot, axis=-1) - 1
        own_index = slot_of * capacity + rank_in
        outputs = returned.reshape(-1, model_width)[own_index].reshape(
            row_count, top_count, model_width
        )
        moe_sum = jnp.einsum("rk,rkd->rd", gate_weights, outputs.astype(jnp.float32))
    hidden_out = hidden_mid + moe_sum
    normed_out = rms_scale(hidden_out, post_gain)
    return (hidden_out, normed_out)


def solution(mesh):
    in_specs = (
        P("expert", "tensor"),
        P("tensor", None),
        P(("expert", "tensor"), None),
        P(),
        P(),
        P("expert", None),
        P(),
        P("expert", None, None, "tensor"),
        P(),
    )
    out_specs = (P(("expert", "tensor"), None), P(("expert", "tensor"), None))
    return jax.shard_map(
        on_device, mesh=mesh, in_specs=in_specs, out_specs=out_specs, check_vma=False
    )
```

profile of v0, /device:TPU:0, one launch (start us, length us, event | category | flops | bytes accessed | tf_op | source)
XLA Modules:
  0.0 380.9 jit_solution(10148748740071930744)
XLA Ops:
  7.2 1.5 copy-done
  8.8 2.7 convolution_convert_fusion.1
  11.4 4.2 %all-to-all-start = ((bf16[4,64,2048]{2,1,0:T(8,128)(2,1)}), bf16[4,64,2048]{2,1,0:T(8,128)(2,1)S(1)}, u32[]{:S(2)}, u32[]{:S(2)}) async-start(bf16[4,64,2048]{2,1,0:T(8,128)(2,1)} %bitcast), calls=%async_computation | async-start | bytes 2097152 | tf_op jit(solution)/shard_map/all_to_all | solution.py:52
  15.7 0.8 fusion.66
  16.5 13.6 %all-to-all-done = bf16[4,64,2048]{2,1,0:T(8,128)(2,1)S(1)} async-done(((bf16[4,64,2048]{2,1,0:T(8,128)(2,1)}), bf16[4,64,2048]{2,1,0:T(8,128)(2,1)S(1)}, u32[]{:S(2)}, u32[]{:S(2)}) %all-to-all-start) | async-done | bytes 1048608 | tf_op jit(solution)/shard_map/all_to_all | solution.py:52
  30.3 1.1 multiply_reduce_fusion.1
  31.4 1.1 fusion.41
  36.2 79.1 %all-gather.2.cloned.1.call-done = bf16[2048,2176]{1,0:T(8,128)(2,1)} async-done(((bf16[64,2176]{1,0:T(8,128)(2,1)}), bf16[2048,2176]{1,0:T(8,128)(2,1)}) %all-gather.2.cloned.1.call-update) | async-done | bytes 8912912 | tf_op jit(solution)/shard_map/all_gather | solution.py:74
  115.3 2.1 fusion.67
  117.5 3.5 fusion.18
  121.0 1.0 copy.55
  122.1 8.8 %fusion.21 = (bf16[32,64,64]{2,1,0:T(8,128)(2,1)}, bf16[32,64,64]{2,1,0:T(8,128)(2,1)S(1)}) fusion(s32[32,64,8]{2,1,0:T(8,128)S(1)} %get-tuple-element.10, bf16[32,64,8]{2,1,0:T(8,128)(2,1)S(1)} %get-tuple-element.9, bf16[32,64,8]{2,1,0:T(8,128)(2,1)S(1)} %get-tuple-element.8), kind=kLoop, calls=%fused_computation.23 | loop fusion | flops 4980736 | bytes 655360 | tf_op jit(solution)/shard_map/reduce_sum | solution.py:94
  130.9 1.3 copy.56
  132.2 1.1 convert_element_type.89
  133.3 1.0 copy.57
  134.3 1.7 fusion.33
  136.5 13.4 %convolution_convert_fusion = bf16[32,16,10,2048]{3,1,2,0:T(8,128)(2,1)} fusion(bf16[32,64,2176]{2,1,0:T(8,128)(2,1)} %bitcast.79, f32[32,64,16]{1,2,0:T(8,128)S(1)} %get-tuple-element.12, f32[32,64,16]{1,2,0:T(8,128)S(1)} %copy.61), kind=kOutput, calls=%fused_computation.11 | convolution fusion | flops 1353318400 | bytes 29622272 | tf_op jit(solution)/shard_map/busr,bud->bsrd/dot_general | solution.py:110
  149.9 0.8 fusion.26
  151.2 46.3 %fusion.8 = f32[8,4,16,10,2,256]{5,3,4,1,0,2:T(8,128)} fusion(bf16[16,3,2048,256]{3,2,1,0:T(8,128)(2,1)} %param.16, bf16[8,4,16,10,2048,1]{4,2,3,1,0,5:T(8,128)(2,1)} %bitcast.76), kind=kOutput, calls=%fused_computation.12 | convolution fusion | flops 10737418240 | bytes 65011712 | tf_op jit(solution)/shard_map/nqsmd,scdf->nqsmcf/dot_general | solution.py:15
  197.5 23.3 %convert_bitcast_fusion = bf16[8,4,16,10,2048]{4,3,1,0,2:T(8,128)(2,1)} fusion(bf16[16,3,2048,256]{3,2,1,0:T(8,128)(2,1)} %param.16, f32[8,4,16,10,2,256]{5,3,4,1,0,2:T(8,128)} %fusion.8, f32[8,4,16,10]{3,1,0,2:T(4,128)S(1)} %copy.64), kind=kOutput, calls=%fused_computation.4 | convolution fusion | flops 5388369920 | bytes 54546432 | tf_op jit(solution)/shard_map/nqsmf,sdf->nqsmd/dot_general | solution.py:22
  220.8 27.4 %bitcast_convert_fusion = bf16[4,8,64,2048]{3,2,1,0:T(8,128)(2,1)} fusion(bf16[8,4,16,10,2048]{4,3,1,0,2:T(8,128)(2,1)} %convert_bitcast_fusion, f32[8,4,64,16]{2,3,0,1:T(8,128)S(1)} %copy.59, f32[8,4,64,16]{2,3,1,0:T(8,128)S(1)} %bitcast.80), kind=kOutput, calls=%fused_computation.9 | convolution fusion | flops 1347026944 | bytes 29622272 | tf_op jit(solution)/shard_map/hqusr,hqsrd->qhud/dot_general | solution.py:122
  248.3 70.5 %reduce-scatter.2.cloned.1.call-done = bf16[512,2048]{1,0:T(8,128)(2,1)} async-done(((bf16[2048,2048]{1,0:T(8,128)(2,1)}), bf16[512,2048]{1,0:T(8,128)(2,1)}) %reduce-scatter.2.cloned.1.call-update) | async-done | bytes 2097168 | tf_op jit(solution)/shard_map/reduce_scatter | solution.py:128
  318.8 53.7 %all_to_all.10 = bf16[8,64,2048]{2,1,0:T(8,128)(2,1)S(1)} all-to-all(bf16[8,64,2048]{2,1,0:T(8,128)(2,1)} %bitcast.83), channel_id=1, replica_groups=mesh['expert'=8,'tensor'=4] {'expert'}, dimensions={0} | all-to-all | bytes 4194304 | tf_op jit(solution)/shard_map/all_to_all | solution.py:134
  373.1 0.9 multiply_multiply_fusion
  (53 shorter events, 5.4 us)
Async XLA Ops:
  7.2 1.6 copy-start
  7.2 25.3 %copy-start.2 = (bf16[64,2048]{1,0:T(8,128)(2,1)S(1)}, bf16[64,2048]{1,0:T(8,128)(2,1)}, u32[]{:S(2)}) copy-start(bf16[64,2048]{1,0:T(8,128)(2,1)} %param.11) | copy-start | bytes 786436
  7.2 25.3 %copy-start.5 = (f32[2048]{0:T(1024)S(1)}, f32[2048]{0:T(1024)}, u32[]{:S(2)}) copy-start(f32[2048]{0:T(1024)} %param.12) | copy-start | bytes 24580
  7.2 25.3 %copy-start.4 = (f32[2048,64]{0,1:T(8,128)S(1)}, f32[2048,64]{0,1:T(8,128)}, u32[]{:S(2)}) copy-start(f32[2048,64]{0,1:T(8,128)} %param.13) | copy-start | bytes 1572868
  7.2 27.4 %copy-start.7 = (s32[128]{0:T(128)S(1)}, s32[128]{0:T(128)}, u32[]{:S(2)}) copy-start(s32[128]{0:T(128)} %param.15) | copy-start | bytes 1540
  11.4 18.7 %all-to-all-start = ((bf16[4,64,2048]{2,1,0:T(8,128)(2,1)}), bf16[4,64,2048]{2,1,0:T(8,128)(2,1)S(1)}, u32[]{:S(2)}, u32[]{:S(2)}) async-start(bf16[4,64,2048]{2,1,0:T(8,128)(2,1)} %bitcast), calls=%async_computation | async-start | bytes 2097152 | tf_op jit(solution)/shard_map/all_to_all | solution.py:52
  15.7 99.7 %all-gather.2.cloned.1.call-start = ((), (), s32[]{:S(2)}) async-start(), calls=%async_computation.3 | async-start | bytes 9191424 | tf_op jit(solution)/shard_map/all_gather | solution.py:74
  34.5 284.3 %reduce-scatter.2.cloned.1.call-start = ((), (), s32[]{:S(2)}) async-start(), calls=%async_computation.4 | async-start | bytes 10485760 | tf_op jit(solution)/shard_map/reduce_scatter | solution.py:128
  248.2 125.8 %copy-start.1 = (bf16[512,2048]{1,0:T(8,128)(2,1)S(1)}, bf16[512,2048]{1,0:T(8,128)(2,1)}, u32[]{:S(2)}) copy-start(bf16[512,2048]{1,0:T(8,128)(2,1)} %param.10) | copy-start | bytes 6291460
  248.3 124.9 %copy-start.6 = (f32[2048]{0:T(1024)S(1)}, f32[2048]{0:T(1024)}, u32[]{:S(2)}) copy-start(f32[2048]{0:T(1024)} %param.17) | copy-start | bytes 24580
  373.1 1.0 copy-start.3
Sparse Core Ops, SparseCore 0:
  34.6 80.6 all-gather.1
  248.4 70.3 reduce-scatter.1
where the time goes:
time: 381 us
  waiting for transfers between devices  163 us (43%)
  matrix products  116 us (30%)
  blocking collectives  53.7 us (14%)
  other arithmetic  23.2 us (6%)
  between operations  14.3 us (4%)
  local copies, waits for them, and re-layouts  6.49 us (2%)
  starting transfers between devices  4.28 us (1%)
    all_gather x1, waiting for transfers between devices, on_device(): lax.all_gather(jnp.concatenate([normed, side], axis=1), ('expert', 'tenso...  79.1 us
    reduce_scatter x1, waiting for transfers between devices, on_device(): lax.psum_scatter(combined.astype(jnp.bfloat16).reshape(-1, model_width),...  70.5 us
    all_to_all x1, blocking collectives, on_device(): lax.all_to_all(moe_sum, 'expert', split_axis=0, concat_axis=0, tiled=True)  53.7 us
    dot_general x1, matrix products, expert_inner(): jnp.einsum('nqsmd,scdf->nqsmcf', block_rows, weights[:, :2], preferred_el...  46.3 us
    dot_general x1, matrix products, on_device(): jnp.einsum('hqusr,hqsrd->qhud', pick_hot.reshape(holders, groups, row_cou...  27.4 us
    dot_general x1, matrix products, expert_down(): jnp.einsum('nqsmf,sdf->nqsmd', inner_act, weights[:, 2], preferred_elemen...  23.3 us
    all_to_all x1, waiting for transfers between devices, on_device(): lax.all_to_all(jnp.dot(context, out_proj, preferred_element_type=jnp.floa...  13.6 us
    dot_general x1, matrix products, on_device(): jnp.einsum('busr,bud->bsrd', pick_hot, all_rows, preferred_element_type=j...  13.4 us
  transfers between devices with their start and end apart: 3, of which 3 were waited for; matrix products, arithmetic and copies ran while one was open for 1% of the time, Pallas kernels for 0%

commit v1 on v0

--- a/solution.py
+++ b/solution.py
@@ -4,6 +4,28 @@
 from jax.sharding import PartitionSpec as P
 
 EPS = 1e-06
+
+
+def in_order(pieces, dim):
+    pieces = jnp.moveaxis(pieces, 0, dim)
+    shape = pieces.shape
+    return pieces.reshape(*shape[:dim], shape[dim] * shape[dim + 1], *shape[dim + 2 :])
+
+
+def collected_by_bits(array, axis):
+    length = lax.axis_size(axis)
+    parts = array[None]
+    for level in range(length.bit_length() - 1):
+        bit = 1 << level
+        other = lax.ppermute(parts, axis, [(i, i ^ bit) for i in range(length)])
+        both = jnp.stack([parts, other])
+        upper = lax.axis_index(axis) >> level & 1
+        parts = jnp.where(upper == 0, both, both[::-1]).reshape(-1, *array.shape)
+    return parts
+
+
+def collect(x, axis, dim):
+    return in_order(collected_by_bits(x, axis), dim)
 
 
 def rms_scale(values, gain_row):
@@ -71,9 +93,9 @@
     gate_lo = (gate_weights - gate_hi.astype(jnp.float32)).astype(jnp.bfloat16)
     side = jnp.concatenate([own_ids.astype(jnp.bfloat16), gate_hi, gate_lo], axis=1)
     side = jnp.pad(side, ((0, 0), (0, 128 - 3 * top_count)))
-    packed = lax.all_gather(
-        jnp.concatenate([normed, side], axis=1), ("expert", "tensor"), axis=0, tiled=True
-    ).reshape(blocks, row_count, model_width + 128)
+    packed = collect(jnp.concatenate([normed, side], axis=1), ("expert", "tensor"), 0).reshape(
+        blocks, row_count, model_width + 128
+    )
     all_rows = packed[:, :, :model_width]
     all_ids = packed[:, :, model_width : model_width + top_count].astype(jnp.int32)
     all_hi = packed[:, :, model_width + top_count : model_width + 2 * top_count]

time: 381 us -> 615 us (1.61)
  waiting for transfers between devices: 163 us -> 362 us
  other arithmetic: 23.2 us -> 50.3 us
  starting transfers between devices: 4.28 us -> 11.3 us
    ppermute x0 -> x5, waiting for transfers between devices: none -> 276 us  [collected_by_bits(): other = lax.ppermute(parts, axis, [(i, i ^ bit) for i in range(length)])]
    all_gather x1 -> x0, waiting for transfers between devices: 79.1 us -> none  [on_device(): lax.all_gather(jnp.concatenate([normed, side], axis=1), ('expert', 'tenso...]
    select_n x0 -> x4, other arithmetic: none -> 17.8 us  [collected_by_bits(): parts = jnp.where(upper == 0, both, both[::-1]).reshape(-1, *array.shape)]
    another operation x0 -> x7, other arithmetic: none -> 12.5 us  [collected_by_bits(): both = jnp.stack([parts, other])]
    ppermute x0 -> x5, starting transfers between devices: none -> 7.11 us  [collected_by_bits(): other = lax.ppermute(parts, axis, [(i, i ^ bit) for i in range(length)])]
  transfers between devices with their start and end apart: 3 -> 7, of which waited for: 3 -> 7; matrix products, arithmetic and copies ran while one was open for 1% -> 0% of each run, Pallas kernels for 0% -> 0%
where the time goes in v1:
time: 615 us; the launch traced here: 614 us
  waiting for transfers between devices  362 us (59%)
  matrix products  116 us (19%)
  blocking collectives  53.9 us (9%)
  other arithmetic  50.3 us (8%)
  between operations  14.4 us (2%)
  starting transfers between devices  11.3 us (2%)
  local copies, waits for them, and re-layouts  6.5 us (1%)
    ppermute x5, waiting for transfers between devices, collected_by_bits(): other = lax.ppermute(parts, axis, [(i, i ^ bit) for i in range(length)])  276 us
    reduce_scatter x1, waiting for transfers between devices, on_device(): lax.psum_scatter(combined.astype(jnp.bfloat16).reshape(-1, model_width),...  71.7 us
    all_to_all x1, blocking collectives, on_device(): lax.all_to_all(moe_sum, 'expert', split_axis=0, concat_axis=0, tiled=True)  53.9 us
    dot_general x1, matrix products, expert_inner(): jnp.einsum('nqsmd,scdf->nqsmcf', block_rows, weights[:, :2], preferred_el...  46.4 us
    dot_general x1, matrix products, on_device(): jnp.einsum('hqusr,hqsrd->qhud', pick_hot.reshape(holders, groups, row_cou...  27.4 us
    dot_general x1, matrix products, expert_down(): jnp.einsum('nqsmf,sdf->nqsmd', inner_act, weights[:, 2], preferred_elemen...  23.3 us
    select_n x4, other arithmetic, collected_by_bits(): parts = jnp.where(upper == 0, both, both[::-1]).reshape(-1, *array.shape)  17.8 us
    all_to_all x1, waiting for transfers between devices, on_device(): lax.all_to_all(jnp.dot(context, out_proj, preferred_element_type=jnp.floa...  14.3 us
  transfers between devices with their start and end apart: 7, of which 7 were waited for; matrix products, arithmetic and copies ran while one was open for 0% of the time, Pallas kernels for 0%

profile of v1, /device:TPU:0, one launch (start us, length us, event | category | flops | bytes accessed | tf_op | source)
XLA Modules:
  0.0 614.0 jit_solution(6006784594999195469)
XLA Ops:
  8.8 2.7 convolution_convert_fusion.1
  11.4 4.2 all-to-all-start
  15.8 14.3 %all-to-all-done = bf16[4,64,2048]{2,1,0:T(8,128)(2,1)S(1)} async-done(((bf16[4,64,2048]{2,1,0:T(8,128)(2,1)}), bf16[4,64,2048]{2,1,0:T(8,128)(2,1)S(1)}, u32[]{:S(2)}, u32[]{:S(2)}) %all-to-all-start) | async-done | bytes 1048608 | tf_op jit(solution)/shard_map/all_to_all | solution.py:74
  34.1 14.3 %collective-permute-done.1 = bf16[2,64,2176]{2,1,0:T(8,128)(2,1)S(1)} collective-permute-done((bf16[2,64,2176]{2,1,0:T(8,128)(2,1)S(1)}, bf16[2,64,2176]{2,1,0:T(8,128)(2,1)S(1)}, u32[]{:S(2)}, u32[]{:S(2)}) %collective-permute-start.1) | collective-permute-done | bytes 557088 | tf_op jit(solution)/shard_map/ppermute | solution.py:20
  48.7 2.3 collective-permute-start.2
  51.0 24.1 %collective-permute-done.2 = bf16[4,64,2176]{2,1,0:T(8,128)(2,1)} collective-permute-done((bf16[4,64,2176]{2,1,0:T(8,128)(2,1)S(1)}, bf16[4,64,2176]{2,1,0:T(8,128)(2,1)}, u32[]{:S(2)}, u32[]{:S(2)}) %collective-permute-start.2) | collective-permute-done | bytes 1114144 | tf_op jit(solution)/shard_map/ppermute | solution.py:20
  76.6 1.9 reverse_select_fusion.2
  78.5 1.8 collective-permute-start.3
  80.3 47.5 %collective-permute-done.3 = bf16[8,64,2176]{2,1,0:T(8,128)(2,1)} collective-permute-done((bf16[8,64,2176]{2,1,0:T(8,128)(2,1)}, bf16[8,64,2176]{2,1,0:T(8,128)(2,1)}, u32[]{:S(2)}, u32[]{:S(2)}) %collective-permute-start.3) | collective-permute-done | bytes 2228256 | tf_op jit(solution)/shard_map/ppermute | solution.py:20
  127.8 2.7 pad_maximum_fusion.1
  130.6 3.1 reverse_select_fusion.1
  133.7 2.5 collective-permute-start.4
  137.8 188.4 %collective-permute-done.4 = bf16[16,64,2176]{2,1,0:T(8,128)(2,1)} collective-permute-done((bf16[16,64,2176]{2,1,0:T(8,128)(2,1)}, bf16[16,64,2176]{2,1,0:T(8,128)(2,1)}, u32[]{:S(2)}, u32[]{:S(2)}) %collective-permute-start.4) | collective-permute-done | bytes 4456480 | tf_op jit(solution)/shard_map/ppermute | solution.py:20
  326.2 7.9 %pad_maximum_fusion = bf16[2,16,64,2176]{3,2,1,0:T(8,128)(2,1)} fusion(bf16[1,16,64,2176]{3,2,1,0:T(8,128)(2,1)} %bitcast.15, bf16[1,16,64,2176]{3,2,1,0:T(8,128)(2,1)} %bitcast.13), kind=kLoop, calls=%fused_computation.13 | loop fusion | flops 4456448 | bytes 17825792 | tf_op jit(solution)/shard_map/stack | solution.py:21
  334.2 12.7 %reverse_select_fusion = bf16[2,16,64,2176]{3,2,1,0:T(8,128)(2,1)} fusion(bf16[2,16,64,2176]{3,2,1,0:T(8,128)(2,1)} %pad_maximum_fusion, pred[]{:T(512)S(6)} %eq.122), kind=kLoop, calls=%fused_computation.12 | loop fusion | flops 4456448 | bytes 17825792 | tf_op jit(solution)/shard_map/jit(_where)/select_n | solution.py:23
  346.8 2.1 fusion.71
  349.0 3.7 fusion.18
  353.7 8.8 %fusion.21 = (bf16[32,64,64]{2,1,0:T(8,128)(2,1)}, bf16[32,64,64]{2,1,0:T(8,128)(2,1)S(1)}) fusion(s32[32,64,8]{2,1,0:T(8,128)S(1)} %get-tuple-element.10, bf16[32,64,8]{2,1,0:T(8,128)(2,1)S(1)} %get-tuple-element.9, bf16[32,64,8]{2,1,0:T(8,128)(2,1)S(1)} %get-tuple-element.8), kind=kLoop, calls=%fused_computation.27 | loop fusion | flops 4980736 | bytes 655360 | tf_op jit(solution)/shard_map/reduce_sum | solution.py:116
  368.2 13.4 %convolution_convert_fusion = bf16[32,16,10,2048]{3,1,2,0:T(8,128)(2,1)} fusion(bf16[32,64,2176]{2,1,0:T(8,128)(2,1)} %bitcast.96, f32[32,64,16]{1,2,0:T(8,128)S(1)} %get-tuple-element.14, f32[32,64,16]{1,2,0:T(8,128)S(1)} %copy.61), kind=kOutput, calls=%fused_computation.11 | convolution fusion | flops 1353318400 | bytes 29622272 | tf_op jit(solution)/shard_map/busr,bud->bsrd/dot_general | solution.py:132
  382.8 46.4 %fusion.8 = f32[8,4,16,10,2,256]{5,3,4,1,0,2:T(8,128)} fusion(bf16[16,3,2048,256]{3,2,1,0:T(8,128)(2,1)} %param.16, bf16[8,4,16,10,2048,1]{4,2,3,1,0,5:T(8,128)(2,1)} %bitcast.97), kind=kOutput, calls=%fused_computation.14 | convolution fusion | flops 10737418240 | bytes 65011712 | tf_op jit(solution)/shard_map/nqsmd,scdf->nqsmcf/dot_general | solution.py:37
  429.2 23.3 %convert_bitcast_fusion = bf16[8,4,16,10,2048]{4,3,1,0,2:T(8,128)(2,1)} fusion(bf16[16,3,2048,256]{3,2,1,0:T(8,128)(2,1)} %param.16, f32[8,4,16,10,2,256]{5,3,4,1,0,2:T(8,128)} %fusion.8, f32[8,4,16,10]{3,1,0,2:T(4,128)S(1)} %copy.64), kind=kOutput, calls=%fused_computation.4 | convolution fusion | flops 5388369920 | bytes 54546432 | tf_op jit(solution)/shard_map/nqsmf,sdf->nqsmd/dot_general | solution.py:44
  452.5 27.4 %bitcast_convert_fusion = bf16[4,8,64,2048]{3,2,1,0:T(8,128)(2,1)} fusion(bf16[8,4,16,10,2048]{4,3,1,0,2:T(8,128)(2,1)} %convert_bitcast_fusion, f32[8,4,64,16]{2,3,0,1:T(8,128)S(1)} %copy.59, f32[8,4,64,16]{2,3,1,0:T(8,128)S(1)} %bitcast.101), kind=kOutput, calls=%fused_computation.9 | convolution fusion | flops 1347026944 | bytes 29622272 | tf_op jit(solution)/shard_map/hqusr,hqsrd->qhud/dot_general | solution.py:144
  480.0 71.7 %reduce-scatter.2.cloned.1.call-done = bf16[512,2048]{1,0:T(8,128)(2,1)} async-done(((bf16[2048,2048]{1,0:T(8,128)(2,1)}), bf16[512,2048]{1,0:T(8,128)(2,1)}) %reduce-scatter.2.cloned.1.call-update) | async-done | bytes 2097168 | tf_op jit(solution)/shard_map/reduce_scatter | solution.py:150
  551.7 53.9 %all_to_all.10 = bf16[8,64,2048]{2,1,0:T(8,128)(2,1)S(1)} all-to-all(bf16[8,64,2048]{2,1,0:T(8,128)(2,1)} %bitcast.104), channel_id=1, replica_groups=mesh['expert'=8,'tensor'=4] {'expert'}, dimensions={0} | all-to-all | bytes 4194304 | tf_op jit(solution)/shard_map/all_to_all | solution.py:156
  (72 shorter events, 18.4 us)
Async XLA Ops:
  7.2 1.6 copy-start
  7.2 8.5 %copy-start.7 = (s32[256,8]{0,1:T(8,128)S(1)}, s32[256,8]{0,1:T(8,128)}, u32[]{:S(2)}) copy-start(s32[256,8]{0,1:T(8,128)} %param.14) | copy-start | bytes 24580
  7.2 23.1 %copy-start.2 = (bf16[64,2048]{1,0:T(8,128)(2,1)S(1)}, bf16[64,2048]{1,0:T(8,128)(2,1)}, u32[]{:S(2)}) copy-start(bf16[64,2048]{1,0:T(8,128)(2,1)} %param.11) | copy-start | bytes 786436
  7.2 23.3 %copy-start.5 = (f32[2048]{0:T(1024)S(1)}, f32[2048]{0:T(1024)}, u32[]{:S(2)}) copy-start(f32[2048]{0:T(1024)} %param.12) | copy-start | bytes 24580
  7.2 23.4 %copy-start.4 = (f32[2048,64]{0,1:T(8,128)S(1)}, f32[2048,64]{0,1:T(8,128)}, u32[]{:S(2)}) copy-start(f32[2048,64]{0,1:T(8,128)} %param.13) | copy-start | bytes 1572868
  11.4 18.7 %all-to-all-start = ((bf16[4,64,2048]{2,1,0:T(8,128)(2,1)}), bf16[4,64,2048]{2,1,0:T(8,128)(2,1)S(1)}, u32[]{:S(2)}, u32[]{:S(2)}) async-start(bf16[4,64,2048]{2,1,0:T(8,128)(2,1)} %bitcast), calls=%async_computation | async-start | bytes 2097152 | tf_op jit(solution)/shard_map/all_to_all | solution.py:74
  15.7 536.0 %reduce-scatter.2.cloned.1.call-start = ((), (), s32[]{:S(2)}) async-start(), calls=%async_computation.3 | async-start | bytes 10485760 | tf_op jit(solution)/shard_map/reduce_scatter | solution.py:150
  31.9 1.6 collective-permute-start
  33.7 14.7 %collective-permute-start.1 = (bf16[2,64,2176]{2,1,0:T(8,128)(2,1)S(1)}, bf16[2,64,2176]{2,1,0:T(8,128)(2,1)S(1)}, u32[]{:S(2)}, u32[]{:S(2)}) collective-permute-start(bf16[2,64,2176]{2,1,0:T(8,128)(2,1)S(1)} %get-tuple-element.12), channel_id=1, source_target_pairs={{0,2},{1,3},{2,0},{3,1},{4,6},{5,7},{6,4},{7,5},{8,10},{9,11},{10,... | collective-permute-start | bytes 1671176 | tf_op jit(solution)/shard_map/ppermute | solution.py:20
  48.7 26.4 %collective-permute-start.2 = (bf16[4,64,2176]{2,1,0:T(8,128)(2,1)S(1)}, bf16[4,64,2176]{2,1,0:T(8,128)(2,1)}, u32[]{:S(2)}, u32[]{:S(2)}) collective-permute-start(bf16[4,64,2176]{2,1,0:T(8,128)(2,1)S(1)} %bitcast.99), channel_id=1, source_target_pairs={{0,4},{1,5},{2,6},{3,7},{4,0},{5,1},{6,2},{7,3},{8,12},{9,13},{10,... | collective-permute-start | bytes 3342344 | tf_op jit(solution)/shard_map/ppermute | solution.py:20
  78.5 49.3 %collective-permute-start.3 = (bf16[8,64,2176]{2,1,0:T(8,128)(2,1)}, bf16[8,64,2176]{2,1,0:T(8,128)(2,1)}, u32[]{:S(2)}, u32[]{:S(2)}) collective-permute-start(bf16[8,64,2176]{2,1,0:T(8,128)(2,1)} %bitcast.11), channel_id=1, source_target_pairs={{0,8},{1,9},{2,10},{3,11},{4,12},{5,13},{6,14},{7,15},{8,0},{9,1},... | collective-permute-start | bytes 6684680 | tf_op jit(solution)/shard_map/ppermute | solution.py:20
  130.5 5.7 copy-start.8
  133.7 192.6 %collective-permute-start.4 = (bf16[16,64,2176]{2,1,0:T(8,128)(2,1)}, bf16[16,64,2176]{2,1,0:T(8,128)(2,1)}, u32[]{:S(2)}, u32[]{:S(2)}) collective-permute-start(bf16[16,64,2176]{2,1,0:T(8,128)(2,1)} %bitcast.14), channel_id=1, source_target_pairs={{0,16},{1,17},{2,18},{3,19},{4,20},{5,21},{6,22},{7,23},{8,24},{9,... | collective-permute-start | bytes 13369352 | tf_op jit(solution)/shard_map/ppermute | solution.py:20
  480.0 126.2 %copy-start.6 = (f32[2048]{0:T(1024)S(1)}, f32[2048]{0:T(1024)}, u32[]{:S(2)}) copy-start(f32[2048]{0:T(1024)} %param.17) | copy-start | bytes 24580
  551.7 55.4 %copy-start.1 = (bf16[512,2048]{1,0:T(8,128)(2,1)S(1)}, bf16[512,2048]{1,0:T(8,128)(2,1)}, u32[]{:S(2)}) copy-start(bf16[512,2048]{1,0:T(8,128)(2,1)} %param.10) | copy-start | bytes 6291460
  606.2 1.0 copy-start.3
Sparse Core Ops, SparseCore 0:
  480.1 71.5 reduce-scatter.1
